TPU v7x, 128 devices: a whole 4x4x4 slice. The times are simulated.
128 devices in a mesh: req: 32 (over y, z_lo, x), exp: 4 (over z_hi, core).
Axes of the slice: x: 4, y: 4, z: 4 (z_hi: 2, z_lo: 2; z = z_hi * 2 + z_lo), core: 2. Of those that a mesh axis runs over, the one named last changes fastest.
Arguments:
- activations: bfloat16 [16384, 1536], P('req'), may hold values from -6 to 6
- attn_gain: float32 [1536], replicated, may hold values from 0.1 to 1.9
- w_query: bfloat16 [1536, 1536], P(None, 'exp'), may hold values from -0.15625 to 0.15625
- key_value_weight: bfloat16 [1536, 2, 256], replicated, may hold values from -0.15625 to 0.15625
- w_output: bfloat16 [1536, 1536], P('exp'), may hold values from -0.15625 to 0.15625
- group_prefix_cache: bfloat16 [8192, 2, 2, 128], P('req')
- lengths: int32 [64], replicated, may hold values from 64 to 448, as said below
- groups: int32 [64], replicated, may hold values from 0 to 3
- owners: int32 [32], replicated, may hold values from 0 to 31, each once
- moe_gain: float32 [1536], replicated, may hold values from 0.1 to 1.9
- w_gate: bfloat16 [32, 1536, 768], P('req', None, 'exp'), may hold values from -0.15625 to 0.15625
- w_up: bfloat16 [32, 1536, 768], P('req', None, 'exp'), may hold values from -0.15625 to 0.15625
- w_down: bfloat16 [32, 768, 1536], P('req', 'exp'), may hold values from -0.21875 to 0.21875
- picks: int32 [16384, 4], P('req'), may hold values from 0 to 31, all different within a row; in each aligned block of 512 rows (0 to 511, 512 to 1023, ...) at most 128 rows name the same one
- pick_weight: float32 [16384, 4], P('req'), may hold values from 0.05 to 0.6
Outputs:
- out: bfloat16 [16384, 1536], P('req')
Inputs may be any that keep to these rules, and one draw needn't show every extreme that they name: `lengths`: entries 2r and 2r+1 sum to 512; every entry is a multiple of 64. `owners`: each value appears once. `picks`: a row names 4 different experts; in the rows of one index of req no expert is named by more than 128 rows.
All inputs are finite; a program needn't handle non-finite values.
Results may differ from a plain program's by a relative error of at most 0.0073.
Values may be sent and summed in bfloat16 or wider, within the bound.
No kernel may reach another device: no remote copies, remote signals or barrier semaphores. Data moves between devices by JAX's collectives and lax.ppermute only.
A program may use at most 128 MiB of HBM per device.

v0:
```python
import jax
import jax.numpy as jnp
from jax import lax
from jax.sharding import PartitionSpec as P

QUERY_HEADS = 12
KEY_VALUE_HEADS = 2
HEAD_SIZE = 128
TOP = 4
GROUPS = 4
REQ_DEV = 2
LMIN = 64


EPS = 1e-06


def rms_scale(rows, gain):
    rows32 = rows.astype(jnp.float32)
    inverse = lax.rsqrt(jnp.mean(rows32 * rows32, axis=-1, keepdims=True) + EPS)
    return (rows32 * inverse * gain).astype(jnp.bfloat16)


def prefix_for(gathered, owners, group, per_group):
    prefix_segments = lax.dynamic_slice_in_dim(owners, group * per_group, per_group, 0)
    return gathered[prefix_segments].reshape(per_group * gathered.shape[1], 2, gathered.shape[3])


def slots_hidden(block, gate_w, up_w):
    rows = block.reshape(-1, block.shape[2])
    gate = jnp.dot(rows, gate_w, preferred_element_type=jnp.float32)
    up = jnp.dot(rows, up_w, preferred_element_type=jnp.float32)
    hidden = (jnp.maximum(gate, 0.0) * up).astype(jnp.bfloat16)
    return hidden.reshape(block.shape[0], block.shape[1], gate_w.shape[1])


def body(
    activations,
    attn_gain,
    w_query,
    key_value_weight,
    w_output,
    group_prefix_cache,
    lengths,
    groups,
    owners,
    moe_gain,
    w_gate,
    w_up,
    w_down,
    picks,
    pick_weight,
):
    req_index = lax.axis_index("req")
    expert_index = lax.axis_index("exp")
    n_req = lax.axis_size("req")
    n_exp = lax.axis_size("exp")
    tok = activations.shape[0]
    heads_per_shard = w_query.shape[1] // HEAD_SIZE
    key_value_head = expert_index * heads_per_shard // (QUERY_HEADS // KEY_VALUE_HEADS)
    normalized_input = rms_scale(activations, attn_gain)
    query_rows = (
        jnp.dot(normalized_input, w_query, preferred_element_type=jnp.float32) * HEAD_SIZE ** (-0.5)
    ).astype(jnp.bfloat16)
    query_rows = query_rows.reshape(tok, heads_per_shard, HEAD_SIZE)
    kv_weight = lax.dynamic_slice_in_dim(key_value_weight, key_value_head * HEAD_SIZE, HEAD_SIZE, 2)
    local_key_value = jnp.einsum(
        "td,dcf->tcf", normalized_input, kv_weight, preferred_element_type=jnp.float32
    ).astype(jnp.bfloat16)
    own_piece = lax.dynamic_index_in_dim(group_prefix_cache, key_value_head, 2, keepdims=False)
    gathered = lax.all_gather(own_piece, "req", axis=0, tiled=True).reshape(
        n_req, own_piece.shape[0], 2, HEAD_SIZE
    )
    pair = lax.dynamic_slice_in_dim(lengths, req_index * REQ_DEV, REQ_DEV, 0)
    pair_groups = lax.dynamic_slice_in_dim(groups, req_index * REQ_DEV, REQ_DEV, 0)
    per_group = n_req // GROUPS
    positions = jnp.arange(tok)
    in_first = positions < pair[0]
    blocks = tok // LMIN
    prefixes = jnp.stack(
        [
            prefix_for(gathered, owners, pair_groups[0], per_group),
            prefix_for(gathered, owners, pair_groups[1], per_group),
        ]
    )
    block_req = (jnp.arange(blocks) * LMIN >= pair[0]).astype(jnp.int32)
    block_prefix = prefixes[block_req]
    prefix_len = block_prefix.shape[1]
    block_queries = query_rows.reshape(blocks, LMIN, heads_per_shard, HEAD_SIZE)
    pre_scores = jnp.einsum(
        "bthd,bpd->hbtp", block_queries, block_prefix[:, :, 0], preferred_element_type=jnp.float32
    )
    pre_scores = pre_scores.reshape(heads_per_shard, tok, prefix_len)
    suf_scores = jnp.einsum(
        "thd,sd->hts", query_rows, local_key_value[:, 0], preferred_element_type=jnp.float32
    )
    allowed = (positions[None, :] <= positions[:, None]) & (in_first[:, None] == in_first[None, :])
    suf_scores = jnp.where(allowed[None], suf_scores, -jnp.inf)
    top = jnp.maximum(
        jnp.max(pre_scores, axis=-1, keepdims=True), jnp.max(suf_scores, axis=-1, keepdims=True)
    )
    pre_exp = jnp.exp(pre_scores - top)
    suf_exp = jnp.exp(suf_scores - top)
    denom = jnp.sum(pre_exp, axis=-1, keepdims=True) + jnp.sum(suf_exp, axis=-1, keepdims=True)
    pre_w = (
        (pre_exp / denom).astype(jnp.bfloat16).reshape(heads_per_shard, blocks, LMIN, prefix_len)
    )
    suf_w = (suf_exp / denom).astype(jnp.bfloat16)
    pre_ctx = jnp.einsum(
        "hbtp,bpd->bthd", pre_w, block_prefix[:, :, 1], preferred_element_type=jnp.float32
    )
    suf_ctx = jnp.einsum(
        "hts,sd->thd", suf_w, local_key_value[:, 1], preferred_element_type=jnp.float32
    )
    context = (pre_ctx.reshape(tok, heads_per_shard, HEAD_SIZE) + suf_ctx).astype(jnp.bfloat16)
    context = context.reshape(tok, heads_per_shard * HEAD_SIZE)
    attn = lax.psum(jnp.dot(context, w_output, preferred_element_type=jnp.float32), "exp")
    resid = (activations.astype(jnp.float32) + attn).astype(jnp.bfloat16)
    normed_moe = rms_scale(resid, moe_gain)
    width_model = normed_moe.shape[1]
    cap = min(tok, 2 * tok * TOP // n_req)
    quarter = cap // n_exp
    flat = picks.reshape(-1)
    onehot = (flat[:, None] == jnp.arange(n_req, dtype=jnp.int32)[None, :]).astype(jnp.int32)
    before = jnp.cumsum(onehot, axis=0) - onehot
    slot = jnp.sum(before * onehot, axis=1)
    row_of = jnp.arange(tok * TOP) // TOP
    send = jnp.zeros((cap, n_req, width_model), jnp.bfloat16).at[slot, flat].set(normed_moe[row_of])
    gate_weight = w_gate[0]
    up_weight = w_up[0]
    down_weight = w_down[0]
    received = lax.all_to_all(send, "req", split_axis=1, concat_axis=1, tiled=True)
    hidden = slots_hidden(received, gate_weight, up_weight)
    part = lax.psum_scatter(
        jnp.einsum("snf,fd->snd", hidden, down_weight, preferred_element_type=jnp.float32),
        "exp",
        scatter_dimension=0,
        tiled=True,
    ).astype(jnp.bfloat16)
    back = lax.all_to_all(part, "req", split_axis=1, concat_axis=1, tiled=True)
    local = slot - expert_index * quarter
    keep = (local >= 0) & (local < quarter)
    picked = (
        back[jnp.clip(local, 0, quarter - 1), flat]
        .astype(jnp.float32)
        .reshape(tok, TOP, width_model)
    )
    weights_kept = jnp.where(keep.reshape(tok, TOP), pick_weight, 0.0)
    mix = jnp.sum(weights_kept[:, :, None] * picked, axis=1)
    total = lax.psum(mix, "exp")
    return (resid.astype(jnp.float32) + total).astype(jnp.bfloat16)


def solution(mesh):
    return jax.shard_map(
        body,
        mesh=mesh,
        in_specs=(
            P("req", None),
            P(),
            P(None, "exp"),
            P(),
            P("exp", None),
            P("req", None, None, None),
            P(),
            P(),
            P(),
            P(),
            P("req", None, "exp"),
            P("req", None, "exp"),
            P("req", "exp", None),
            P("req", None),
            P("req", None),
        ),
        out_specs=P("req", None),
        check_vma=False,
    )
```

profile of v0, /device:TPU:3, one launch (start us, length us, event | category | flops | bytes accessed | tf_op | source)
XLA Modules:
  0.0 936.8 jit_solution(13483857162273876479)
XLA Ops:
  13.8 2.8 fusion.26
  20.1 2.3 fusion.16
  22.6 124.3 %all-gather.3.cloned.1.call-done = bf16[8192,2,1,128]{3,0,1,2:T(8,128)(2,1)} async-done(((bf16[256,2,1,128]{3,0,1,2:T(8,128)(2,1)}), bf16[8192,2,1,128]{3,0,1,2:T(8,128)(2,1)}) %all-gather.3.cloned.1.call-update) | async-done | bytes 4194320 | tf_op jit(solution)/shard_map/all_gather | solution.py:71
  147.0 2.9 gather_fusion
  150.0 2.9 gather_fusion.1
  153.2 4.7 gather_fusion.2
  157.9 8.6 bitcast_reduce_fusion
  166.6 6.6 fusion.1
  174.0 7.7 fusion.24
  184.9 2.3 fusion.27
  187.2 2.7 fusion.51
  191.3 9.2 reduce-window.6
  201.7 85.7 %all-reduce.3.cloned.1.call-done = f32[512,1536]{1,0:T(8,128)} async-done(((f32[512,1536]{1,0:T(8,128)}), f32[512,1536]{1,0:T(8,128)}) %all-reduce.3.cloned.1.call-update) | async-done | bytes 3145744 | tf_op jit(solution)/shard_map/psum | solution.py:117
  287.5 2.4 fusion.12
  291.5 38.3 %scatter_custom_fusion = bf16[4096,1536]{1,0:T(8,128)(2,1)} fusion(s32[2048]{0:T(1024)S(1)} %get-tuple-element.21, bf16[512,1536]{1,0:T(8,128)(2,1)S(1)} %fusion.14, s32[2048]{0:T(1024)S(1)} %get-tuple-element.20, bf16[]{:T(256)} %constant.81.clone.1), kind=kCustom, calls=%fused_computation.12 | custom fusion | bytes 12582914
  329.8 12.3 %copy.97 = bf16[128,32,1536]{2,0,1:T(8,128)(2,1)S(1)} copy(bf16[128,32,1536]{2,1,0:T(8,128)(2,1)} %bitcast.130) | data formatting | bytes 25165824 | tf_op jit(solution)/shard_map/scatter | solution.py:128
  342.2 153.4 %all_to_all.10 = bf16[128,32,1536]{2,0,1:T(8,128)(2,1)S(1)} all-to-all(bf16[128,32,1536]{2,0,1:T(8,128)(2,1)S(1)} %copy.97), channel_id=1, replica_groups=mesh['req'=32,'exp'=4] {'req'}, dimensions={1} | all-to-all | bytes 25165824 | tf_op jit(solution)/shard_map/all_to_all | solution.py:132
  495.6 24.0 %copy.98 = bf16[128,32,1536]{2,1,0:T(8,128)(2,1)S(1)} copy(bf16[128,32,1536]{2,0,1:T(8,128)(2,1)S(1)} %all_to_all.10) | data formatting | bytes 25165824 | tf_op jit(solution)/shard_map/all_to_all | solution.py:132
  519.6 4.2 convolution_maximum_fusion
  523.9 5.3 fusion.6
  529.2 3.2 copy.99
  532.4 10.4 %fusion.18 = f32[128,32,1536]{2,0,1:T(8,128)} fusion(bf16[128,32,192]{2,1,0:T(8,128)(2,1)S(1)} %bitcast.131, bf16[1,192,1536]{2,1,0:T(8,128)(2,1)S(1)} %copy-done.11), kind=kOutput, calls=%fused_computation.42 | convolution fusion | flops 2415919104 | bytes 27328512 | tf_op jit(solution)/shard_map/snf,fd->snd/dot_general | solution.py:135
  542.8 188.3 %reduce-scatter.2.cloned.1.call-done = f32[32,32,1536]{2,0,1:T(8,128)} async-done(((f32[128,32,1536]{2,0,1:T(8,128)}), f32[32,32,1536]{2,0,1:T(8,128)}) %reduce-scatter.2.cloned.1.call-update) | async-done | bytes 6291472 | tf_op jit(solution)/shard_map/reduce_scatter | solution.py:134
  731.1 4.9 convert_element_type.80
  736.1 7.1 all-to-all-start.1
  743.7 41.7 %all-to-all-done.1 = bf16[32,32,1536]{2,0,1:T(8,128)(2,1)} async-done(((bf16[32,32,1536]{2,0,1:T(8,128)(2,1)}), bf16[32,32,1536]{2,0,1:T(8,128)(2,1)}, u32[]{:S(2)}, u32[]{:S(2)}) %all-to-all-start.1) | async-done | bytes 3145760 | tf_op jit(solution)/shard_map/all_to_all | solution.py:140
  785.4 3.6 copy.101
  789.1 37.6 %gather_fusion.3 = bf16[2048,1536]{1,0:T(8,128)(2,1)} fusion(bf16[32,32,1536]{2,1,0:T(8,128)(2,1)S(1)} %copy.101, s32[2048]{0:T(1024)S(1)} %bitcast.129), kind=kCustom, calls=%fused_computation.4 | custom fusion | bytes 12599296 | tf_op jit(solution)/shard_map/gather | solution.py:144
  826.6 12.2 %reshape.289 = f32[512,4,1536]{2,1,0:T(4,128)} reshape(bf16[2048,1536]{1,0:T(8,128)(2,1)} %gather_fusion.3) | data formatting | bytes 18874368 | tf_op jit(solution)/shard_map/convert_element_type | solution.py:145
  838.9 12.8 %multiply_reduce_fusion = f32[512,1536]{1,0:T(8,128)} fusion(f32[512,4,1536]{2,1,0:T(4,128)} %reshape.289, f32[512,4]{1,0:T(8,128)S(1)} %broadcast_select_fusion), kind=kLoop, calls=%fused_computation.9 | loop fusion | flops 5505024 | bytes 15736832 | tf_op jit(solution)/shard_map/reduce_sum | solution.py:149
  851.7 74.8 %all-reduce.5.cloned.1.call-done = f32[512,1536]{1,0:T(8,128)} async-done(((f32[512,1536]{1,0:T(8,128)}), f32[512,1536]{1,0:T(8,128)}) %all-reduce.5.cloned.1.call-update) | async-done | bytes 3145744 | tf_op jit(solution)/shard_map/psum | solution.py:150
  926.5 3.5 fusion.15
  (105 shorter events, 18.6 us)
Async XLA Ops:
  6.5 11.4 %copy-start = (bf16[1536,2,256]{2,1,0:T(2,128)(2,1)S(1)}, bf16[1536,2,256]{2,1,0:T(2,128)(2,1)}, u32[]{:S(2)}) copy-start(bf16[1536,2,256]{2,1,0:T(2,128)(2,1)} %param.18) | copy-start | bytes 4718596
  6.5 140.4 %all-gather.3.cloned.1.call-start = ((), (), s32[]{:S(2)}) async-start(), calls=%async_computation.6 | async-start | bytes 4325376 | tf_op jit(solution)/shard_map/all_gather | solution.py:71
  8.6 278.9 %all-reduce.3.cloned.1.call-start = ((), (), s32[]{:S(2)}) async-start(), calls=%async_computation.3 | async-start | bytes 6291456 | tf_op jit(solution)/shard_map/psum | solution.py:117
  13.8 5.6 copy-start.5
  13.8 5.6 copy-start.21
  16.6 1.3 copy-start.8
  19.1 1.0 copy-start.9
  20.0 2.4 copy-start.12
  20.0 2.5 copy-start.16
  153.2 4.7 copy-start.7
  166.6 6.7 copy-start.4
  184.9 2.3 copy-start.10
  189.9 0.7 copy-start.14
  189.9 11.5 %copy-start.18 = (s32[2]{0:T(128)S(1)}, s32[2]{0:T(128)}, u32[]{:S(2)}) copy-start(s32[2]{0:T(128)} %constant.87) | copy-start | bytes 28
  189.9 11.6 %copy-start.17 = (s32[2]{0:T(128)S(1)}, s32[2]{0:T(128)}, u32[]{:S(2)}) copy-start(s32[2]{0:T(128)} %constant.90) | copy-start | bytes 28
  189.9 97.5 %copy-start.6 = (bf16[512,1536]{1,0:T(8,128)(2,1)S(1)}, bf16[512,1536]{1,0:T(8,128)(2,1)}, u32[]{:S(2)}) copy-start(bf16[512,1536]{1,0:T(8,128)(2,1)} %param.15) | copy-start | bytes 4718596
  190.0 541.2 %reduce-scatter.2.cloned.1.call-start = ((), (), s32[]{:S(2)}) async-start(), calls=%async_computation.4 | async-start | bytes 31457280 | tf_op jit(solution)/shard_map/reduce_scatter | solution.py:134
  201.7 89.4 %copy-start.13 = (f32[1536]{0:T(1024)S(1)}, f32[1536]{0:T(1024)}, u32[]{:S(2)}) copy-start(f32[1536]{0:T(1024)} %param.24) | copy-start | bytes 18436
  289.9 1.2 copy-start.2
  495.6 24.0 %copy-start.19 = (bf16[1,1536,192]{1,2,0:T(8,128)(2,1)S(1)}, bf16[1,1536,192]{1,2,0:T(8,128)(2,1)}, u32[]{:S(2)}) copy-start(bf16[1,1536,192]{1,2,0:T(8,128)(2,1)} %param.25) | copy-start | bytes 1769476
  519.6 4.3 copy-start.20
  529.2 3.2 copy-start.11
  736.1 7.5 copy-start.15
  736.1 49.4 %all-to-all-start.1 = ((bf16[32,32,1536]{2,0,1:T(8,128)(2,1)}), bf16[32,32,1536]{2,0,1:T(8,128)(2,1)}, u32[]{:S(2)}, u32[]{:S(2)}) async-start(bf16[32,32,1536]{2,0,1:T(8,128)(2,1)} %convert_element_type.80), calls=%async_computation.2 | async-start | bytes 6291456 | tf_op jit(solution)/shard_map/all_to_all | solution.py:140
  743.2 183.3 %all-reduce.5.cloned.1.call-start = ((), (), s32[]{:S(2)}) async-start(), calls=%async_computation.5 | async-start | bytes 6291456 | tf_op jit(solution)/shard_map/psum | solution.py:150
  851.6 74.8 %copy-start.3 = (bf16[512,1536]{1,0:T(8,128)(2,1)S(1)}, bf16[512,1536]{1,0:T(8,128)(2,1)}, u32[]{:S(2)}) copy-start(bf16[512,1536]{1,0:T(8,128)(2,1)} %copy-done.2) | copy-start | bytes 4718596
  851.7 78.3 %copy-start.1 = (bf16[1536,2,256]{2,1,0:T(2,128)(2,1)S(1)}, bf16[1536,2,256]{2,1,0:T(2,128)(2,1)}, u32[]{:S(2)}) copy-start(bf16[1536,2,256]{2,1,0:T(2,128)(2,1)} %param.18) | copy-start | bytes 4718596
Sparse Core Ops, SparseCore 0:
  9.0 137.9 all-gather.2
  190.1 97.3 all-reduce.2
  542.9 188.1 reduce-scatter.1
  851.8 74.6 all-reduce.4
where the time goes:
time: 941 us; the launch traced here: 937 us
  waiting for transfers between devices  515 us (55%)
  local copies, waits for them, and re-layouts  155 us (16%)
  blocking collectives  153 us (16%)
  matrix products  46.9 us (5%)
  other arithmetic  43.6 us (5%)
  between operations  15.2 us (2%)
    reduce_scatter x1, waiting for transfers between devices, body(): lax.psum_scatter(jnp.einsum('snf,fd->snd', hidden, down_weight, preferred...  188 us
    all_to_all x1, blocking collectives, body(): lax.all_to_all(send, 'req', split_axis=1, concat_axis=1, tiled=True)  153 us
    all_gather x1, waiting for transfers between devices, body(): lax.all_gather(own_piece, 'req', axis=0, tiled=True)  124 us
    psum x1, waiting for transfers between devices, body(): lax.psum(jnp.dot(context, w_output, preferred_element_type=jnp.float32),...  85.7 us
    psum x1, waiting for transfers between devices, body(): total = lax.psum(mix, 'exp')  74.8 us
    all_to_all x1, waiting for transfers between devices, body(): back = lax.all_to_all(part, 'req', split_axis=1, concat_axis=1, tiled=True)  41.7 us
    unnamed x48, local copies, waits for them, and re-layouts  41.3 us
    gather x1, local copies, waits for them, and re-layouts, body(): back[jnp.clip(local, 0, quarter - 1), flat].astype(jnp.float32)  37.6 us
  transfers between devices with their start and end apart: 5, of which 5 were waited for; matrix products, arithmetic and copies ran while one was open for 3% of the time, Pallas kernels for 0%

commit v1 on v0

v1 whole, which is shorter than its diff:
```python
import jax
import jax.numpy as jnp
from jax import lax
from jax.sharding import PartitionSpec as P

QUERY_HEADS = 12
KEY_VALUE_HEADS = 2
HEAD_SIZE = 128
TOP = 4
GROUPS = 4
REQ_DEV = 2
LMIN = 64


EPS = 1e-06


def rms_scale(rows, gain):
    rows32 = rows.astype(jnp.float32)
    inverse = lax.rsqrt(jnp.mean(rows32 * rows32, axis=-1, keepdims=True) + EPS)
    return (rows32 * inverse * gain).astype(jnp.bfloat16)


def prefix_for(gathered, owners, group, per_group):
    prefix_segments = lax.dynamic_slice_in_dim(owners, group * per_group, per_group, 0)
    return gathered[prefix_segments].reshape(per_group * gathered.shape[1], 2, gathered.shape[3])


def body(
    activations,
    attn_gain,
    w_query,
    key_value_weight,
    w_output,
    group_prefix_cache,
    lengths,
    groups,
    owners,
    moe_gain,
    w_gate,
    w_up,
    w_down,
    picks,
    pick_weight,
):
    req_index = lax.axis_index("req")
    expert_index = lax.axis_index("exp")
    n_req = lax.axis_size("req")
    n_exp = lax.axis_size("exp")
    tok = activations.shape[0]
    width_model = activations.shape[1]
    heads_per_shard = w_query.shape[1] // HEAD_SIZE
    key_value_head = expert_index * heads_per_shard // (QUERY_HEADS // KEY_VALUE_HEADS)

    own_piece = lax.dynamic_index_in_dim(group_prefix_cache, key_value_head, 2, keepdims=False)
    gathered = lax.all_gather(own_piece, "req", axis=0, tiled=False)
    w_output_full = lax.all_gather(w_output, "exp", axis=0, tiled=True)
    gate_full = lax.all_gather(w_gate[0], "exp", axis=1, tiled=True)
    up_full = lax.all_gather(w_up[0], "exp", axis=1, tiled=True)
    down_full = lax.all_gather(w_down[0], "exp", axis=0, tiled=True)

    normalized_input = rms_scale(activations, attn_gain)
    query_rows = (
        jnp.dot(normalized_input, w_query, preferred_element_type=jnp.float32) * HEAD_SIZE ** (-0.5)
    ).astype(jnp.bfloat16)
    query_rows = query_rows.reshape(tok, heads_per_shard, HEAD_SIZE)
    kv_weight = lax.dynamic_slice_in_dim(key_value_weight, key_value_head * HEAD_SIZE, HEAD_SIZE, 2)
    local_key_value = jnp.einsum(
        "td,dcf->tcf", normalized_input, kv_weight, preferred_element_type=jnp.float32
    ).astype(jnp.bfloat16)

    pair = lax.dynamic_slice_in_dim(lengths, req_index * REQ_DEV, REQ_DEV, 0)
    pair_groups = lax.dynamic_slice_in_dim(groups, req_index * REQ_DEV, REQ_DEV, 0)
    per_group = n_req // GROUPS
    positions = jnp.arange(tok)
    in_first = positions < pair[0]
    prefix_a = prefix_for(gathered, owners, pair_groups[0], per_group)
    prefix_b = prefix_for(gathered, owners, pair_groups[1], per_group)
    zero_q = jnp.zeros_like(query_rows)
    first3 = in_first[:, None, None]
    query_ab = jnp.concatenate(
        [jnp.where(first3, query_rows, zero_q), jnp.where(first3, zero_q, query_rows)], axis=-1
    )
    keys_ab = jnp.concatenate([prefix_a[:, 0], prefix_b[:, 0]], axis=-1)
    values_ab = jnp.concatenate([prefix_a[:, 1], prefix_b[:, 1]], axis=-1)
    pre_scores = jnp.einsum("thd,pd->htp", query_ab, keys_ab, preferred_element_type=jnp.float32)
    suf_scores = jnp.einsum(
        "thd,sd->hts", query_rows, local_key_value[:, 0], preferred_element_type=jnp.float32
    )
    allowed = (positions[None, :] <= positions[:, None]) & (in_first[:, None] == in_first[None, :])
    suf_scores = jnp.where(allowed[None], suf_scores, -jnp.inf)
    top = jnp.maximum(
        jnp.max(pre_scores, axis=-1, keepdims=True), jnp.max(suf_scores, axis=-1, keepdims=True)
    )
    pre_exp = jnp.exp(pre_scores - top)
    suf_exp = jnp.exp(suf_scores - top)
    denom = jnp.sum(pre_exp, axis=-1, keepdims=True) + jnp.sum(suf_exp, axis=-1, keepdims=True)
    pre_w = (pre_exp / denom).astype(jnp.bfloat16)
    suf_w = (suf_exp / denom).astype(jnp.bfloat16)
    pre_ctx_ab = jnp.einsum("htp,pd->thd", pre_w, values_ab, preferred_element_type=jnp.float32)
    pre_ctx = jnp.where(first3, pre_ctx_ab[..., :HEAD_SIZE], pre_ctx_ab[..., HEAD_SIZE:])
    suf_ctx = jnp.einsum(
        "hts,sd->thd", suf_w, local_key_value[:, 1], preferred_element_type=jnp.float32
    )
    context = (pre_ctx + suf_ctx).astype(jnp.bfloat16)
    context = context.reshape(tok, heads_per_shard * HEAD_SIZE)
    context_full = lax.all_gather(context, "exp", axis=1, tiled=True)
    attn = jnp.dot(context_full, w_output_full, preferred_element_type=jnp.float32)
    resid = (activations.astype(jnp.float32) + attn).astype(jnp.bfloat16)
    normed_moe = rms_scale(resid, moe_gain)

    n_experts = n_req
    cap = min(tok, 2 * tok * TOP // n_req)
    quarter = cap // n_exp
    expert_ids = jnp.arange(n_experts, dtype=jnp.int32)
    chose = jnp.any(picks[:, :, None] == expert_ids[None, None, :], axis=1).astype(jnp.bfloat16)
    earlier = (positions[None, :] < positions[:, None]).astype(jnp.bfloat16)
    before = jnp.dot(earlier, chose, preferred_element_type=jnp.float32).astype(jnp.int32)
    slot = jnp.take_along_axis(before, picks, axis=1)
    local = slot - expert_index * quarter
    keep = (local >= 0) & (local < quarter)
    target = jnp.where(keep, picks * quarter + local, -1)
    columns = jnp.arange(n_experts * quarter, dtype=jnp.int32)
    hits = target[:, :, None] == columns[None, None, :]
    dispatch = jnp.any(hits, axis=1).astype(jnp.bfloat16)
    send = jnp.einsum("tq,td->qd", dispatch, normed_moe, preferred_element_type=jnp.float32)
    send = send.astype(jnp.bfloat16).reshape(n_experts, quarter, width_model)
    received = lax.all_to_all(send, "req", split_axis=0, concat_axis=0, tiled=True)
    rows = received.reshape(-1, width_model)
    gate = jnp.dot(rows, gate_full, preferred_element_type=jnp.float32)
    up = jnp.dot(rows, up_full, preferred_element_type=jnp.float32)
    hidden = (jnp.maximum(gate, 0.0) * up).astype(jnp.bfloat16)
    part = jnp.dot(hidden, down_full, preferred_element_type=jnp.float32).astype(jnp.bfloat16)
    part = part.reshape(n_experts, quarter, width_model)
    back = lax.all_to_all(part, "req", split_axis=0, concat_axis=0, tiled=True)
    back = back.reshape(-1, width_model)
    combine = jnp.sum(jnp.where(hits, pick_weight[:, :, None], 0.0), axis=1)
    combine_hi = combine.astype(jnp.bfloat16)
    combine_lo = (combine - combine_hi.astype(jnp.float32)).astype(jnp.bfloat16)
    mix = jnp.dot(combine_hi, back, preferred_element_type=jnp.float32) + jnp.dot(
        combine_lo, back, preferred_element_type=jnp.float32
    )
    total = lax.psum(mix, "exp")
    return (resid.astype(jnp.float32) + total).astype(jnp.bfloat16)


def solution(mesh):
    return jax.shard_map(
        body,
        mesh=mesh,
        in_specs=(
            P("req", None),
            P(),
            P(None, "exp"),
            P(),
            P("exp", None),
            P("req", None, None, None),
            P(),
            P(),
            P(),
            P(),
            P("req", None, "exp"),
            P("req", None, "exp"),
            P("req", "exp", None),
            P("req", None),
            P("req", None),
        ),
        out_specs=P("req", None),
        check_vma=False,
    )
```

time: 941 us -> 512 us (0.54)
  blocking collectives: 153 us -> 0 us
  waiting for transfers between devices: 515 us -> 377 us
  local copies, waits for them, and re-layouts: 155 us -> 44.3 us
  other arithmetic: 43.6 us -> 13.6 us
    reduce_scatter x1 -> x0, waiting for transfers between devices: 188 us -> none  [body(): lax.psum_scatter(jnp.einsum('snf,fd->snd', hidden, down_weight, preferred...]
    all_to_all x1 -> x0, blocking collectives: 153 us -> none  [body(): lax.all_to_all(send, 'req', split_axis=1, concat_axis=1, tiled=True)]
    all_gather x1 -> x6, waiting for transfers between devices: 124 us -> 261 us  [the longest x1 124 us: body(): gathered = lax.all_gather(own_piece, 'req', axis=0, tiled=False)]
    psum x1 -> x0, waiting for transfers between devices: 85.7 us -> none  [body(): lax.psum(jnp.dot(context, w_output, preferred_element_type=jnp.float32),...]
    unnamed x48 -> x38, local copies, waits for them, and re-layouts: 41.3 us -> 1.58 us
    all_to_all x2 -> x0, local copies, waits for them, and re-layouts: 27.6 us -> none  [the longest x1 24 us: body(): lax.all_to_all(send, 'req', split_axis=1, concat_axis=1, tiled=True)]
    gather x2 -> x3, local copies, waits for them, and re-layouts: 42.2 us -> 17.2 us  [body(): slot = jnp.take_along_axis(before, picks, axis=1)]
    convert_element_type x2 -> x1, local copies, waits for them, and re-layouts: 15.4 us -> 1.91 us  [body(): context = (pre_ctx + suf_ctx).astype(jnp.bfloat16)]
  transfers between devices with their start and end apart: 5 -> 9, of which waited for: 5 -> 8; matrix products, arithmetic and copies ran while one was open for 3% -> 15% of each run, Pallas kernels for 0% -> 0%
where the time goes in v1:
time: 512 us; the launch traced here: 510 us
  waiting for transfers between devices  377 us (74%)
  matrix products  45 us (9%)
  local copies, waits for them, and re-layouts  44.3 us (9%)
  between operations  15.2 us (3%)
  starting transfers between devices  14.7 us (3%)
  other arithmetic  13.6 us (3%)
    all_gather x1, waiting for transfers between devices, body(): gathered = lax.all_gather(own_piece, 'req', axis=0, tiled=False)  124 us
    psum x1, waiting for transfers between devices, body(): total = lax.psum(mix, 'exp')  74.6 us
    all_gather x1, waiting for transfers between devices, body(): up_full = lax.all_gather(w_up[0], 'exp', axis=1, tiled=True)  45.7 us
    all_to_all x1, waiting for transfers between devices, body(): back = lax.all_to_all(part, 'req', split_axis=0, concat_axis=0, tiled=True)  40 us
    all_gather x1, waiting for transfers between devices, body(): down_full = lax.all_gather(w_down[0], 'exp', axis=0, tiled=True)  29 us
    all_gather x1, waiting for transfers between devices, body(): context_full = lax.all_gather(context, 'exp', axis=1, tiled=True)  24.7 us
    all_gather x1, waiting for transfers between devices, body(): gate_full = lax.all_gather(w_gate[0], 'exp', axis=1, tiled=True)  23 us
    gather x3, local copies, waits for them, and re-layouts, body(): slot = jnp.take_along_axis(before, picks, axis=1)  17.2 us
  transfers between devices with their start and end apart: 9, of which 8 were waited for; matrix products, arithmetic and copies ran while one was open for 15% of the time, Pallas kernels for 0%

profile of v1, /device:TPU:3, one launch (start us, length us, event | category | flops | bytes accessed | tf_op | source)
XLA Modules:
  0.0 510.0 jit_solution(1063333685752200654)
XLA Ops:
  6.6 1.4 constant_dynamic-slice_fusion.1
  13.9 2.2 fusion.30
  18.6 2.1 broadcast_select_fusion.1
  23.3 123.7 %all-gather.15.cloned.1.call-done = bf16[8192,2,1,128]{3,0,1,2:T(8,128)(2,1)} async-done(((bf16[256,2,1,128]{3,0,1,2:T(8,128)(2,1)}), bf16[8192,2,1,128]{3,0,1,2:T(8,128)(2,1)}) %all-gather.15.cloned.1.call-update) | async-done | bytes 4194320 | tf_op jit(solution)/shard_map/all_gather | solution.py:56
  147.0 4.8 copy.55
  151.7 3.8 gather_fusion
  155.6 2.3 copy.56
  157.9 3.8 gather_fusion.1
  164.5 1.8 bitcast_reduce_fusion
  166.9 1.7 fusion.1
  168.6 3.5 fusion.27
  172.1 1.9 fusion.31
  174.0 1.9 copy.69
  178.2 16.8 %gather_fusion.2 = s32[2048]{0:T(1024)S(1)} fusion(s32[512,32]{0,1:T(8,128)S(1)} %convolution_convert_fusion.2, s32[2048]{0:T(1024)S(1)} %reshape.148), kind=kCustom, calls=%fused_computation.2 | custom fusion | bytes 32768 | tf_op jit(solution)/shard_map/jit(take_along_axis)/gather | solution.py:119
  195.7 1.6 fusion.2
  197.3 14.6 %all-gather.13.cloned.1.call-done = bf16[1536,1536]{1,0:T(8,128)(2,1)} async-done(((bf16[384,1536]{1,0:T(8,128)(2,1)}), bf16[1536,1536]{1,0:T(8,128)(2,1)}) %all-gather.13.cloned.1.call-update) | async-done | bytes 4718608 | tf_op jit(solution)/shard_map/all_gather | solution.py:57
  211.9 24.7 %all-gather.11.cloned.1.call-done = bf16[512,1536]{0,1:T(8,128)(2,1)} async-done(((bf16[512,384]{0,1:T(8,128)(2,1)}), bf16[512,1536]{0,1:T(8,128)(2,1)}) %all-gather.11.cloned.1.call-update) | async-done | bytes 1572880 | tf_op jit(solution)/shard_map/all_gather | solution.py:107
  236.6 5.7 %fusion.7 = (f32[512]{0:T(512)S(1)}, bf16[512,1536]{1,0:T(8,128)(2,1)S(1)}) fusion(bf16[512,1536]{0,1:T(8,128)(2,1)} %all-gather.11.cloned.1.call-done, bf16[1536,1536]{1,0:T(8,128)(2,1)} %all-gather.13.cloned.1.call-done, bf16[512,1536]{1,0:T(8,128)(2,1)S(1)} %copy-done.4), kind=kOutput, calls=%fused_computation.24 | convolution fusion | flops 2420637184 | bytes 9439232 | tf_op jit(solution)/shard_map/dot_general | solution.py:108
  242.3 3.6 convolution_convert_fusion.1
  246.0 6.9 %all-to-all-start = ((bf16[32,32,1536]{2,1,0:T(8,128)(2,1)}), bf16[32,32,1536]{2,1,0:T(8,128)(2,1)S(1)}, u32[]{:S(2)}, u32[]{:S(2)}) async-start(bf16[32,32,1536]{2,1,0:T(8,128)(2,1)} %bitcast.114), calls=%async_computation | async-start | bytes 6291456 | tf_op jit(solution)/shard_map/all_to_all | solution.py:128
  253.5 45.7 %all-gather.19.cloned.1.call-done = bf16[1,1536,768]{1,2,0:T(8,128)(2,1)} async-done(((bf16[1,1536,192]{1,2,0:T(8,128)(2,1)}), bf16[1,1536,768]{1,2,0:T(8,128)(2,1)}) %all-gather.19.cloned.1.call-update) | async-done | bytes 2359312 | tf_op jit(solution)/shard_map/all_gather | solution.py:59
  299.3 5.9 %fusion.15 = f32[1024,768]{1,0:T(8,128)} fusion(bf16[1024,1536]{1,0:T(8,128)(2,1)S(1)} %bitcast.112, bf16[1,1536,768]{1,2,0:T(8,128)(2,1)} %all-gather.19.cloned.1.call-done), kind=kOutput, calls=%fused_computation.36 | convolution fusion | flops 2415919104 | bytes 8650752 | tf_op jit(solution)/shard_map/dot_general | solution.py:131
  305.2 23.0 %all-gather.17.cloned.1.call-done = bf16[1,1536,768]{1,2,0:T(8,128)(2,1)} async-done(((bf16[1,1536,192]{1,2,0:T(8,128)(2,1)}), bf16[1,1536,768]{1,2,0:T(8,128)(2,1)}) %all-gather.17.cloned.1.call-update) | async-done | bytes 2359312 | tf_op jit(solution)/shard_map/all_gather | solution.py:58
  328.2 29.0 %all-gather.21.cloned.1.call-done = bf16[1,768,1536]{2,1,0:T(8,128)(2,1)} async-done(((bf16[1,192,1536]{2,1,0:T(8,128)(2,1)}), bf16[1,768,1536]{2,1,0:T(8,128)(2,1)}) %all-gather.21.cloned.1.call-update) | async-done | bytes 2359312 | tf_op jit(solution)/shard_map/all_gather | solution.py:60
  357.2 11.0 %convolution_convert_fusion = bf16[1024,1536]{1,0:T(8,128)(2,1)} fusion(bf16[1,768,1536]{2,1,0:T(8,128)(2,1)} %all-gather.21.cloned.1.call-done, f32[1024,768]{1,0:T(8,128)} %fusion.15, bf16[1024,1536]{1,0:T(8,128)(2,1)S(1)} %bitcast.113, bf16[1,1536,768]{1,2,0:T(8,128)(2,1)} %all-gather.17.cloned.1.call-done), kind=kOutput, calls=%fused_computation.18 | convolution fusion | flops 4835770368 | bytes 14155776 | tf_op jit(solution)/shard_map/dot_general | solution.py:133
  368.2 7.1 %all-to-all-start.1 = ((bf16[32,32,1536]{2,1,0:T(8,128)(2,1)}), bf16[32,32,1536]{2,1,0:T(8,128)(2,1)S(1)}, u32[]{:S(2)}, u32[]{:S(2)}) async-start(bf16[32,32,1536]{2,1,0:T(8,128)(2,1)} %bitcast.117), calls=%async_computation.1 | async-start | bytes 6291456 | tf_op jit(solution)/shard_map/all_to_all | solution.py:135
  375.4 2.6 select_reduce_fusion
  378.0 40.0 %all-to-all-done.1 = bf16[32,32,1536]{2,1,0:T(8,128)(2,1)S(1)} async-done(((bf16[32,32,1536]{2,1,0:T(8,128)(2,1)}), bf16[32,32,1536]{2,1,0:T(8,128)(2,1)S(1)}, u32[]{:S(2)}, u32[]{:S(2)}) %all-to-all-start.1) | async-done | bytes 3145760 | tf_op jit(solution)/shard_map/all_to_all | solution.py:135
  418.0 3.5 fusion.48
  421.5 3.5 convolution_add_fusion
  425.1 74.6 %all-reduce.2.cloned.1.call-done = f32[512,1536]{1,0:T(8,128)} async-done(((f32[512,1536]{1,0:T(8,128)}), f32[512,1536]{1,0:T(8,128)}) %all-reduce.2.cloned.1.call-update) | async-done | bytes 3145744 | tf_op jit(solution)/shard_map/psum | solution.py:143
  499.7 3.5 fusion.10
  (85 shorter events, 16.5 us)
Async XLA Ops:
  6.5 11.2 %copy-start = (bf16[1536,2,256]{2,1,0:T(2,128)(2,1)S(1)}, bf16[1536,2,256]{2,1,0:T(2,128)(2,1)}, u32[]{:S(2)}) copy-start(bf16[1536,2,256]{2,1,0:T(2,128)(2,1)} %param.18) | copy-start | bytes 4718596
  6.5 6.9 %copy-start.3 = (bf16[512,1536]{1,0:T(8,128)(2,1)S(1)}, bf16[512,1536]{1,0:T(8,128)(2,1)}, u32[]{:S(2)}) copy-start(bf16[512,1536]{1,0:T(8,128)(2,1)} %param.15) | copy-start | bytes 4718596
  6.5 7.3 %copy-start.16 = (f32[1536]{0:T(1024)S(1)}, f32[1536]{0:T(1024)}, u32[]{:S(2)}) copy-start(f32[1536]{0:T(1024)} %param.16) | copy-start | bytes 18436
  6.5 140.4 %all-gather.15.cloned.1.call-start = ((), (), s32[]{:S(2)}) async-start(), calls=%async_computation.5 | async-start | bytes 4325376 | tf_op jit(solution)/shard_map/all_gather | solution.py:56
  8.7 203.2 %all-gather.13.cloned.1.call-start = ((), (), s32[]{:S(2)}) async-start(), calls=%async_computation.3 | async-start | bytes 5898240 | tf_op jit(solution)/shard_map/all_gather | solution.py:57
  9.4 227.1 %all-gather.11.cloned.1.call-start = ((), (), s32[]{:S(2)}) async-start(), calls=%async_computation.2 | async-start | bytes 1966080 | tf_op jit(solution)/shard_map/all_gather | solution.py:107
  13.8 3.8 copy-start.15
  16.1 1.7 copy-start.7
  18.6 4.1 copy-start.8
  22.0 0.7 copy-start.12
  161.7 2.7 copy-start.9
  161.7 2.7 copy-start.10
  168.6 3.5 copy-start.13
  172.1 5.0 copy-start.11
  176.0 123.3 %all-gather.19.cloned.1.call-start = ((), (), s32[]{:S(2)}) async-start(), calls=%async_computation.7 | async-start | bytes 2949120 | tf_op jit(solution)/shard_map/all_gather | solution.py:59
  176.5 151.7 %all-gather.17.cloned.1.call-start = ((), (), s32[]{:S(2)}) async-start(), calls=%async_computation.6 | async-start | bytes 2949120 | tf_op jit(solution)/shard_map/all_gather | solution.py:58
  178.2 58.3 %copy-start.4 = (bf16[512,1536]{1,0:T(8,128)(2,1)S(1)}, bf16[512,1536]{1,0:T(8,128)(2,1)}, u32[]{:S(2)}) copy-start(bf16[512,1536]{1,0:T(8,128)(2,1)} %param.15) | copy-start | bytes 4718596
  197.3 45.0 %copy-start.17 = (f32[1536]{0:T(1024)S(1)}, f32[1536]{0:T(1024)}, u32[]{:S(2)}) copy-start(f32[1536]{0:T(1024)} %param.24) | copy-start | bytes 18436
  242.3 3.7 copy-start.5
  246.0 53.3 %all-to-all-start = ((bf16[32,32,1536]{2,1,0:T(8,128)(2,1)}), bf16[32,32,1536]{2,1,0:T(8,128)(2,1)S(1)}, u32[]{:S(2)}, u32[]{:S(2)}) async-start(bf16[32,32,1536]{2,1,0:T(8,128)(2,1)} %bitcast.114), calls=%async_computation | async-start | bytes 6291456 | tf_op jit(solution)/shard_map/all_to_all | solution.py:128
  252.9 104.3 %all-gather.21.cloned.1.call-start = ((), (), s32[]{:S(2)}) async-start(), calls=%async_computation.8 | async-start | bytes 2949120 | tf_op jit(solution)/shard_map/all_gather | solution.py:60
  368.2 7.1 %copy-start.14 = (f32[512,4]{0,1:T(4,128)S(1)}, f32[512,4]{0,1:T(4,128)}, u32[]{:S(2)}) copy-start(f32[512,4]{0,1:T(4,128)} %param.29) | copy-start | bytes 24580
  368.2 49.8 %all-to-all-start.1 = ((bf16[32,32,1536]{2,1,0:T(8,128)(2,1)}), bf16[32,32,1536]{2,1,0:T(8,128)(2,1)S(1)}, u32[]{:S(2)}, u32[]{:S(2)}) async-start(bf16[32,32,1536]{2,1,0:T(8,128)(2,1)} %bitcast.117), calls=%async_computation.1 | async-start | bytes 6291456 | tf_op jit(solution)/shard_map/all_to_all | solution.py:135
  375.3 124.4 %all-reduce.2.cloned.1.call-start = ((), (), s32[]{:S(2)}) async-start(), calls=%async_computation.4 | async-start | bytes 6291456 | tf_op jit(solution)/shard_map/psum | solution.py:143
  418.0 3.5 copy-start.2
  425.0 74.6 %copy-start.6 = (bf16[512,1536]{1,0:T(8,128)(2,1)S(1)}, bf16[512,1536]{1,0:T(8,128)(2,1)}, u32[]{:S(2)}) copy-start(bf16[512,1536]{1,0:T(8,128)(2,1)} %copy-done.5) | copy-start | bytes 4718596
  425.1 78.1 %copy-start.1 = (bf16[1536,2,256]{2,1,0:T(2,128)(2,1)S(1)}, bf16[1536,2,256]{2,1,0:T(2,128)(2,1)}, u32[]{:S(2)}) copy-start(bf16[1536,2,256]{2,1,0:T(2,128)(2,1)} %param.18) | copy-start | bytes 4718596
Sparse Core Ops, SparseCore 0:
  9.0 137.9 all-gather.14
  148.6 63.1 all-gather.12
  213.5 22.9 all-gather.10
  238.1 61.1 all-gather.18
  300.8 27.4 all-gather.16
  329.8 27.4 all-gather.20
  425.2 74.4 all-reduce.1

commit v2 on v1

--- a/solution.py
+++ b/solution.py
@@ -24,6 +24,40 @@
 def prefix_for(gathered, owners, group, per_group):
     prefix_segments = lax.dynamic_slice_in_dim(owners, group * per_group, per_group, 0)
     return gathered[prefix_segments].reshape(per_group * gathered.shape[1], 2, gathered.shape[3])
+
+
+def req_shift_pairs(n_req, kind, d):
+    pairs = []
+    for r in range(n_req):
+        if kind == "x":
+            dest = (r // 4) * 4 + (r % 4 + d) % 4
+        elif kind == "z":
+            dest = r ^ 4
+        else:
+            dest = (r + 8 * d) % n_req
+        pairs.append((r, dest))
+    return pairs
+
+
+def exp_flip(x, n_exp, bit):
+    return lax.ppermute(x, "exp", [(e, e ^ bit) for e in range(n_exp)])
+
+
+def gather_exp(x, axis, n_exp):
+    far = exp_flip(x, n_exp, 2)
+    near = exp_flip(jnp.concatenate([x, far], axis=axis), n_exp, 1)
+    return jnp.concatenate([x, far, near], axis=axis)
+
+
+def gather_prefix_halves(mine, n_req):
+    along_x = jnp.stack(
+        [mine] + [lax.ppermute(mine, "req", req_shift_pairs(n_req, "x", d)) for d in (1, 2, 3)]
+    )
+    along_z = jnp.stack([along_x, lax.ppermute(along_x, "req", req_shift_pairs(n_req, "z", 1))])
+    along_y = jnp.stack(
+        [along_z] + [lax.ppermute(along_z, "req", req_shift_pairs(n_req, "y", d)) for d in (1, 2, 3)]
+    )
+    return along_y.reshape((n_req,) + mine.shape)
 
 
 def body(
@@ -53,11 +87,16 @@
     key_value_head = expert_index * heads_per_shard // (QUERY_HEADS // KEY_VALUE_HEADS)
 
     own_piece = lax.dynamic_index_in_dim(group_prefix_cache, key_value_head, 2, keepdims=False)
-    gathered = lax.all_gather(own_piece, "req", axis=0, tiled=False)
-    w_output_full = lax.all_gather(w_output, "exp", axis=0, tiled=True)
-    gate_full = lax.all_gather(w_gate[0], "exp", axis=1, tiled=True)
-    up_full = lax.all_gather(w_up[0], "exp", axis=1, tiled=True)
-    down_full = lax.all_gather(w_down[0], "exp", axis=0, tiled=True)
+    core = expert_index % 2
+    far_half = expert_index // 2
+    half_rows = own_piece.shape[0] // 2
+    mine = lax.dynamic_slice_in_dim(own_piece, core * half_rows, half_rows, 0)
+    halves_mine = gather_prefix_halves(mine, n_req)
+    halves_other = exp_flip(halves_mine, n_exp, 1)
+    w_output_full = gather_exp(w_output, 0, n_exp)
+    gate_full = gather_exp(w_gate[0], 1, n_exp)
+    up_full = gather_exp(w_up[0], 1, n_exp)
+    down_full = gather_exp(w_down[0], 0, n_exp)
 
     normalized_input = rms_scale(activations, attn_gain)
     query_rows = (
@@ -74,8 +113,22 @@
     per_group = n_req // GROUPS
     positions = jnp.arange(tok)
     in_first = positions < pair[0]
-    prefix_a = prefix_for(gathered, owners, pair_groups[0], per_group)
-    prefix_b = prefix_for(gathered, owners, pair_groups[1], per_group)
+    my_y, my_z, my_x = req_index // 8, (req_index // 4) % 2, req_index % 4
+
+    def prefix_of(group):
+        owner = lax.dynamic_slice_in_dim(owners, group * per_group, per_group, 0)
+        where = ((my_y - owner // 8) % 4) * 8 + ((my_z - (owner // 4) % 2) % 2) * 4 + (my_x - owner % 4) % 4
+        part_mine = halves_mine[where]
+        part_other = halves_other[where]
+        rows = jnp.where(
+            core == 0,
+            jnp.concatenate([part_mine, part_other], axis=1),
+            jnp.concatenate([part_other, part_mine], axis=1),
+        )
+        return rows.reshape(per_group * 2 * half_rows, 2, HEAD_SIZE)
+
+    prefix_a = prefix_of(pair_groups[0])
+    prefix_b = prefix_of(pair_groups[1])
     zero_q = jnp.zeros_like(query_rows)
     first3 = in_first[:, None, None]
     query_ab = jnp.concatenate(
@@ -104,7 +157,7 @@
     )
     context = (pre_ctx + suf_ctx).astype(jnp.bfloat16)
     context = context.reshape(tok, heads_per_shard * HEAD_SIZE)
-    context_full = lax.all_gather(context, "exp", axis=1, tiled=True)
+    context_full = gather_exp(context, 1, n_exp)
     attn = jnp.dot(context_full, w_output_full, preferred_element_type=jnp.float32)
     resid = (activations.astype(jnp.float32) + attn).astype(jnp.bfloat16)
     normed_moe = rms_scale(resid, moe_gain)
@@ -140,8 +193,29 @@
     mix = jnp.dot(combine_hi, back, preferred_element_type=jnp.float32) + jnp.dot(
         combine_lo, back, preferred_element_type=jnp.float32
     )
-    total = lax.psum(mix, "exp")
-    return (resid.astype(jnp.float32) + total).astype(jnp.bfloat16)
+    half_tok = tok // 2
+    quarter_tok = tok // 4
+    keep_half = lax.dynamic_slice_in_dim(mix, core * half_tok, half_tok, 0)
+    give_half = lax.dynamic_slice_in_dim(mix, (1 - core) * half_tok, half_tok, 0)
+    half_sum = keep_half + exp_flip(give_half, n_exp, 1)
+    keep_q = lax.dynamic_slice_in_dim(half_sum, far_half * quarter_tok, quarter_tok, 0)
+    give_q = lax.dynamic_slice_in_dim(half_sum, (1 - far_half) * quarter_tok, quarter_tok, 0)
+    quarter_sum = keep_q + exp_flip(give_q, n_exp, 2)
+    my_rows = core * half_tok + far_half * quarter_tok
+    resid_rows = lax.dynamic_slice_in_dim(resid, my_rows, quarter_tok, 0)
+    out_q = (resid_rows.astype(jnp.float32) + quarter_sum).astype(jnp.bfloat16)
+    other_q = exp_flip(out_q, n_exp, 2)
+    out_half = jnp.where(
+        far_half == 0,
+        jnp.concatenate([out_q, other_q], axis=0),
+        jnp.concatenate([other_q, out_q], axis=0),
+    )
+    other_half = exp_flip(out_half, n_exp, 1)
+    return jnp.where(
+        core == 0,
+        jnp.concatenate([out_half, other_half], axis=0),
+        jnp.concatenate([other_half, out_half], axis=0),
+    )
 
 
 def solution(mesh):

time: 512 us -> 359 us (0.70)
  waiting for transfers between devices: 377 us -> 188 us
  starting transfers between devices: 14.7 us -> 49.8 us
  other arithmetic: 13.6 us -> 31.7 us
  between operations: 15.2 us -> 2.47 us
  matrix products: 45 us -> 39.8 us
    all_gather x6 -> x0, waiting for transfers between devices: 261 us -> none  [the longest x1 124 us: body(): gathered = lax.all_gather(own_piece, 'req', axis=0, tiled=False)]
    ppermute x0 -> x22, waiting for transfers between devices: none -> 146 us  [the longest x15 101 us: exp_flip(): return lax.ppermute(x, 'exp', [(e, e ^ bit) for e in range(n_exp)])]
    psum x1 -> x0, waiting for transfers between devices: 74.6 us -> none  [body(): total = lax.psum(mix, 'exp')]
    ppermute x0 -> x22, starting transfers between devices: none -> 37 us  [the longest x15 27.7 us: exp_flip(): return lax.ppermute(x, 'exp', [(e, e ^ bit) for e in range(n_exp)])]
    concatenate x0 -> x5, other arithmetic: none -> 8.02 us  [gather_exp(): near = exp_flip(jnp.concatenate([x, far], axis=axis), n_exp, 1)]
    select_n x1 -> x5, other arithmetic: 0.08 us -> 5.93 us  [the longest x2 3.89 us: prefix_of(): jnp.where(core == 0, jnp.concatenate([part_mine, part_other], axis=1), jn...]
    dot_general x1, matrix products: 11 us -> 5.52 us  [body(): jnp.dot(hidden, down_full, preferred_element_type=jnp.float32)]
  transfers between devices with their start and end apart: 9 -> 24, of which waited for: 8 -> 13; matrix products, arithmetic and copies ran while one was open for 15% -> 23% of each run, Pallas kernels for 0% -> 0%
where the time goes in v2:
time: 359 us; the launch traced here: 353 us
  waiting for transfers between devices  188 us (52%)
  starting transfers between devices  49.8 us (14%)
  local copies, waits for them, and re-layouts  41.3 us (12%)
  matrix products  39.8 us (11%)
  other arithmetic  31.7 us (9%)
    ppermute x15, waiting for transfers between devices, exp_flip(): return lax.ppermute(x, 'exp', [(e, e ^ bit) for e in range(n_exp)])  101 us
    all_to_all x1, waiting for transfers between devices, body(): back = lax.all_to_all(part, 'req', split_axis=0, concat_axis=0, tiled=True)  41.1 us
    ppermute x15, starting transfers between devices, exp_flip(): return lax.ppermute(x, 'exp', [(e, e ^ bit) for e in range(n_exp)])  27.7 us
    ppermute x1, waiting for transfers between devices, gather_prefix_halves(): lax.ppermute(along_x, 'req', req_shift_pairs(n_req, 'z', 1))  24.8 us
    ppermute x3, waiting for transfers between devices, gather_prefix_halves(): lax.ppermute(along_z, 'req', req_shift_pairs(n_req, 'y', d))  20.2 us
    gather x3, local copies, waits for them, and re-layouts, body(): slot = jnp.take_along_axis(before, picks, axis=1)  17.2 us
    concatenate x5, other arithmetic, gather_exp(): near = exp_flip(jnp.concatenate([x, far], axis=axis), n_exp, 1)  8.02 us
    all_to_all x1, starting transfers between devices, body(): back = lax.all_to_all(part, 'req', split_axis=0, concat_axis=0, tiled=True)  7.23 us
  transfers between devices with their start and end apart: 24, of which 13 were waited for; matrix products, arithmetic and copies ran while one was open for 23% of the time, Pallas kernels for 0%

profile of v2, /device:TPU:3, one launch (start us, length us, event | category | flops | bytes accessed | tf_op | source)
XLA Modules:
  0.0 352.6 jit_solution(5521527004541055339)
XLA Ops:
  5.2 3.6 %collective-permute-start.10 = (bf16[384,1536]{1,0:T(8,128)(2,1)}, bf16[384,1536]{1,0:T(8,128)(2,1)}, u32[]{:S(2)}, u32[]{:S(2)}) collective-permute-start(bf16[384,1536]{1,0:T(8,128)(2,1)} %param.19), channel_id=1, source_target_pairs={{0,2},{1,3},{2,0},{3,1},{4,6},{5,7},{6,4},{7,5},{8,10},{9,11},{10,... | collective-permute-start | bytes 3538952 | tf_op jit(solution)/shard_map/ppermute | solution.py:43
  15.1 24.8 %collective-permute-done.3 = bf16[4,128,2,128]{3,1,2,0:T(8,128)(2,1)S(1)} collective-permute-done((bf16[4,128,2,128]{3,1,2,0:T(8,128)(2,1)S(1)}, bf16[4,128,2,128]{3,1,2,0:T(8,128)(2,1)S(1)}, u32[]{:S(2)}, u32[]{:S(2)}) %collective-permute-start.3) | collective-permute-done | bytes 262176 | tf_op jit(solution)/shard_map/ppermute | solution.py:56
  40.0 3.0 collective-permute-start.5
  46.5 6.3 %collective-permute-done.5 = bf16[2,4,128,2,128]{4,2,3,1,0:T(8,128)(2,1)} collective-permute-done((bf16[2,4,128,2,128]{4,2,3,1,0:T(8,128)(2,1)S(1)}, bf16[2,4,128,2,128]{4,2,3,1,0:T(8,128)(2,1)}, u32[]{:S(2)}, u32[]{:S(2)}) %collective-permute-start.5) | collective-permute-done | bytes 524320 | tf_op jit(solution)/shard_map/ppermute | solution.py:58
  52.8 13.1 %collective-permute-done.6 = bf16[2,4,128,2,128]{4,2,3,1,0:T(8,128)(2,1)} collective-permute-done((bf16[2,4,128,2,128]{4,2,3,1,0:T(8,128)(2,1)S(1)}, bf16[2,4,128,2,128]{4,2,3,1,0:T(8,128)(2,1)}, u32[]{:S(2)}, u32[]{:S(2)}) %collective-permute-start.6) | collective-permute-done | bytes 524320 | tf_op jit(solution)/shard_map/ppermute | solution.py:58
  66.7 3.0 pad_maximum_fusion.1
  76.4 3.0 gather_fusion
  79.4 3.0 gather_fusion.2
  82.4 3.2 pad_maximum_fusion
  85.8 3.0 gather_fusion.1
  91.9 3.0 gather_fusion.3
  102.3 3.5 fusion.51
  111.2 9.4 %collective-permute-done.8 = bf16[512,384]{0,1:T(8,128)(2,1)S(1)} collective-permute-done((bf16[512,384]{0,1:T(8,128)(2,1)S(1)}, bf16[512,384]{0,1:T(8,128)(2,1)S(1)}, u32[]{:S(2)}, u32[]{:S(2)}) %collective-permute-start.8) | collective-permute-done | bytes 393248 | tf_op jit(solution)/shard_map/ppermute | solution.py:43
  123.4 16.8 %gather_fusion.4 = s32[2048]{0:T(1024)S(1)} fusion(s32[512,32]{0,1:T(8,128)S(1)} %convolution_convert_fusion.2, s32[2048]{0:T(1024)S(1)} %reshape.171), kind=kCustom, calls=%fused_computation.4 | custom fusion | bytes 32768 | tf_op jit(solution)/shard_map/jit(take_along_axis)/gather | solution.py:172
  142.6 5.6 %fusion.10 = (f32[512]{0:T(512)S(1)}, bf16[512,1536]{1,0:T(8,128)(2,1)S(1)}) fusion(bf16[768,1536]{1,0:T(8,128)(2,1)} %collective-permute-done.11, bf16[384,1536]{1,0:T(8,128)(2,1)} %collective-permute-done.10, bf16[384,1536]{1,0:T(8,128)(2,1)} %param.19, bf16[512,768]{0,1:T(8,128)(2,1)} %collective-permute-done.9, bf16[512,384]{0,1:T(8,128)(2,1)} %copy-done.24, ...), kind=kOutput, calls=%fused_computation.28 | convolution fusion | flops 2439511552 | bytes 9439232 | tf_op jit(solution)/shard_map/dot_general | solution.py:161
  148.2 3.6 %convolution_convert_fusion.1 = bf16[1024,1536]{1,0:T(8,128)(2,1)} fusion(pred[512,1024]{1,0:T(8,128)(4,1)S(1)} %fusion.2, bf16[512,1536]{1,0:T(8,128)(2,1)S(1)} %get-tuple-element.28, f32[1536]{0:T(1024)S(1)} %copy-done.33, f32[512]{0:T(512)S(1)} %add_rsqrt_fusion), kind=kOutput, calls=%fused_computation.26 | convolution fusion | flops 1615331328 | bytes 5251072 | tf_op jit(solution)/shard_map/tq,td->qd/dot_general | solution.py:179
  151.8 5.6 %all-to-all-start = ((bf16[32,32,1536]{2,1,0:T(8,128)(2,1)}), bf16[32,32,1536]{2,1,0:T(8,128)(2,1)S(1)}, u32[]{:S(2)}, u32[]{:S(2)}) async-start(bf16[32,32,1536]{2,1,0:T(8,128)(2,1)} %bitcast.118), calls=%async_computation | async-start | bytes 6291456 | tf_op jit(solution)/shard_map/all_to_all | solution.py:181
  160.5 44.5 %collective-permute-done.12 = bf16[1536,192]{0,1:T(8,128)(2,1)S(1)} collective-permute-done((bf16[1536,192]{0,1:T(8,128)(2,1)}, bf16[1536,192]{0,1:T(8,128)(2,1)S(1)}, u32[]{:S(2)}, u32[]{:S(2)}) %collective-permute-start.12) | collective-permute-done | bytes 589856 | tf_op jit(solution)/shard_map/ppermute | solution.py:43
  210.7 6.9 %collective-permute-done.14 = bf16[1536,192]{0,1:T(8,128)(2,1)S(1)} collective-permute-done((bf16[1536,192]{0,1:T(8,128)(2,1)}, bf16[1536,192]{0,1:T(8,128)(2,1)S(1)}, u32[]{:S(2)}, u32[]{:S(2)}) %collective-permute-start.14) | collective-permute-done | bytes 589856 | tf_op jit(solution)/shard_map/ppermute | solution.py:43
  220.7 9.5 %collective-permute-done.16 = bf16[192,1536]{1,0:T(8,128)(2,1)S(1)} collective-permute-done((bf16[192,1536]{1,0:T(8,128)(2,1)S(1)}, bf16[192,1536]{1,0:T(8,128)(2,1)S(1)}, u32[]{:S(2)}, u32[]{:S(2)}) %collective-permute-start.16) | collective-permute-done | bytes 589856 | tf_op jit(solution)/shard_map/ppermute | solution.py:43
  232.9 4.3 %fusion.21 = f32[1024,768]{1,0:T(8,128)S(1)} fusion(bf16[1024,1536]{1,0:T(8,128)(2,1)S(1)} %bitcast.116, bf16[1536,384]{0,1:T(8,128)(2,1)} %collective-permute-done.13, bf16[1536,192]{0,1:T(8,128)(2,1)} %copy-done.20, bf16[1536,192]{0,1:T(8,128)(2,1)} %bitcast.129), kind=kOutput, calls=%fused_computation.42 | convolution fusion | flops 2422996992 | bytes 8650752 | tf_op jit(solution)/shard_map/dot_general | solution.py:183
  237.3 4.0 %multiply_convert_fusion = bf16[1024,768]{1,0:T(8,128)(2,1)S(1)} fusion(f32[1024,768]{1,0:T(8,128)S(1)} %fusion.21, bf16[1024,1536]{1,0:T(8,128)(2,1)S(1)} %bitcast.117, bf16[1536,384]{0,1:T(8,128)(2,1)} %collective-permute-done.15, bf16[1536,192]{0,1:T(8,128)(2,1)S(1)} %copy-done.19, bf16[1536,192]{0,1:T(8,128)(2,1)S(1)} %bitcast.132), kind=kOutput, calls=%fused_computation.36 | convolution fusion | flops 2425356288 | bytes 10223616 | tf_op jit(solution)/shard_map/dot_general | solution.py:184
  241.4 5.5 %convolution_convert_fusion = bf16[1024,1536]{1,0:T(8,128)(2,1)} fusion(bf16[1024,768]{1,0:T(8,128)(2,1)S(1)} %multiply_convert_fusion, bf16[384,1536]{1,0:T(8,128)(2,1)} %collective-permute-done.17, bf16[192,1536]{1,0:T(8,128)(2,1)S(1)} %copy-done.22, bf16[192,1536]{1,0:T(8,128)(2,1)S(1)} %bitcast.135), kind=kOutput, calls=%fused_computation.25 | convolution fusion | flops 2424569856 | bytes 7077888 | tf_op jit(solution)/shard_map/dot_general | solution.py:186
  246.9 7.2 %all-to-all-start.1 = ((bf16[32,32,1536]{2,1,0:T(8,128)(2,1)}), bf16[32,32,1536]{2,1,0:T(8,128)(2,1)S(1)}, u32[]{:S(2)}, u32[]{:S(2)}) async-start(bf16[32,32,1536]{2,1,0:T(8,128)(2,1)} %bitcast.121), calls=%async_computation.1 | async-start | bytes 6291456 | tf_op jit(solution)/shard_map/all_to_all | solution.py:188
  256.8 41.1 %all-to-all-done.1 = bf16[32,32,1536]{2,1,0:T(8,128)(2,1)S(1)} async-done(((bf16[32,32,1536]{2,1,0:T(8,128)(2,1)}), bf16[32,32,1536]{2,1,0:T(8,128)(2,1)S(1)}, u32[]{:S(2)}, u32[]{:S(2)}) %all-to-all-start.1) | async-done | bytes 3145760 | tf_op jit(solution)/shard_map/all_to_all | solution.py:188
  297.9 3.5 %fusion.70 = f32[512,1536]{1,0:T(8,128)S(1)} fusion(bf16[1024,1536]{1,0:T(8,128)(2,1)S(1)} %bitcast.119, f32[512,1024]{1,0:T(8,128)} %select_reduce_fusion), kind=kOutput, calls=%fused_computation.110 | convolution fusion | flops 1611137024 | bytes 8388608 | tf_op jit(solution)/shard_map/dot_general | solution.py:193
  301.5 3.5 convolution_add_fusion
  308.0 3.0 collective-permute-done.18
  312.8 3.7 %collective-permute-start.19 = (f32[128,1536]{1,0:T(8,128)S(1)}, f32[128,1536]{1,0:T(8,128)S(1)}, u32[]{:S(2)}, u32[]{:S(2)}) collective-permute-start(f32[128,1536]{1,0:T(8,128)S(1)} %constant_dynamic-slice_fusion), channel_id=1, source_target_pairs={{0,2},{1,3},{2,0},{3,1},{4,6},{5,7},{6,4},{7,5},{8,10},{9,11},{10,... | collective-permute-start | bytes 2359304 | tf_op jit(solution)/shard_map/ppermute | solution.py:43
  316.4 17.5 %collective-permute-done.19 = f32[128,1536]{1,0:T(8,128)S(1)} collective-permute-done((f32[128,1536]{1,0:T(8,128)S(1)}, f32[128,1536]{1,0:T(8,128)S(1)}, u32[]{:S(2)}, u32[]{:S(2)}) %collective-permute-start.19) | collective-permute-done | bytes 786464 | tf_op jit(solution)/shard_map/ppermute | solution.py:43
  335.1 2.8 collective-permute-start.20
  337.9 8.5 %collective-permute-done.20 = bf16[128,1536]{1,0:T(8,128)(2,1)S(1)} collective-permute-done((bf16[128,1536]{1,0:T(8,128)(2,1)S(1)}, bf16[128,1536]{1,0:T(8,128)(2,1)S(1)}, u32[]{:S(2)}, u32[]{:S(2)}) %collective-permute-start.20) | collective-permute-done | bytes 393248 | tf_op jit(solution)/shard_map/ppermute | solution.py:43
  (157 shorter events, 70.9 us)
Async XLA Ops:
  0.0 71.6 %copy-start = (bf16[1536,2,256]{2,1,0:T(2,128)(2,1)S(1)}, bf16[1536,2,256]{2,1,0:T(2,128)(2,1)}, u32[]{:S(2)}) copy-start(bf16[1536,2,256]{2,1,0:T(2,128)(2,1)} %param.18) | copy-start | bytes 4718596
  0.0 44.4 %copy-start.32 = (f32[1536]{0:T(1024)S(1)}, f32[1536]{0:T(1024)}, u32[]{:S(2)}) copy-start(f32[1536]{0:T(1024)} %param.16) | copy-start | bytes 18436
  1.2 8.3 %collective-permute-start = (bf16[128,2,128]{2,0,1:T(8,128)(2,1)S(1)}, bf16[128,2,128]{2,0,1:T(8,128)(2,1)S(1)}, u32[]{:S(2)}, u32[]{:S(2)}) collective-permute-start(bf16[128,2,128]{2,0,1:T(8,128)(2,1)S(1)} %bitcast.136), channel_id=1, source_target_pairs={{0,4},{4,8},{8,12},{12,0},{16,20},{20,24},{24,28},{28,16},{32,36},... | collective-permute-start | bytes 196616 | tf_op jit(solution)/shard_map/ppermute | solution.py:54
  2.5 7.0 %collective-permute-start.1 = (bf16[128,2,128]{2,0,1:T(8,128)(2,1)S(1)}, bf16[128,2,128]{2,0,1:T(8,128)(2,1)S(1)}, u32[]{:S(2)}, u32[]{:S(2)}) collective-permute-start(bf16[128,2,128]{2,0,1:T(8,128)(2,1)S(1)} %bitcast.137), channel_id=1, source_target_pairs={{0,8},{4,12},{8,0},{12,4},{16,24},{20,28},{24,16},{28,20},{32,40},... | collective-permute-start | bytes 196616 | tf_op jit(solution)/shard_map/ppermute | solution.py:54
  3.2 6.3 %collective-permute-start.2 = (bf16[128,2,128]{2,0,1:T(8,128)(2,1)S(1)}, bf16[128,2,128]{2,0,1:T(8,128)(2,1)S(1)}, u32[]{:S(2)}, u32[]{:S(2)}) collective-permute-start(bf16[128,2,128]{2,0,1:T(8,128)(2,1)S(1)} %bitcast.138), channel_id=1, source_target_pairs={{0,12},{4,0},{8,4},{12,8},{16,28},{20,16},{24,20},{28,24},{32,44},... | collective-permute-start | bytes 196616 | tf_op jit(solution)/shard_map/ppermute | solution.py:54
  5.2 77.2 %collective-permute-start.10 = (bf16[384,1536]{1,0:T(8,128)(2,1)}, bf16[384,1536]{1,0:T(8,128)(2,1)}, u32[]{:S(2)}, u32[]{:S(2)}) collective-permute-start(bf16[384,1536]{1,0:T(8,128)(2,1)} %param.19), channel_id=1, source_target_pairs={{0,2},{1,3},{2,0},{3,1},{4,6},{5,7},{6,4},{7,5},{8,10},{9,11},{10,... | collective-permute-start | bytes 3538952 | tf_op jit(solution)/shard_map/ppermute | solution.py:43
  9.6 30.3 %collective-permute-start.3 = (bf16[4,128,2,128]{3,1,2,0:T(8,128)(2,1)S(1)}, bf16[4,128,2,128]{3,1,2,0:T(8,128)(2,1)S(1)}, u32[]{:S(2)}, u32[]{:S(2)}) collective-permute-start(bf16[4,128,2,128]{3,1,2,0:T(8,128)(2,1)S(1)} %get-tuple-element.14), channel_id=1, source_target_pairs={{0,16},{4,20},{8,24},{12,28},{16,0},{20,4},{24,8},{28,12},{32,48},... | collective-permute-start | bytes 786440 | tf_op jit(solution)/shard_map/ppermute | solution.py:56
  12.4 32.0 %copy-start.7 = (bf16[512,1536]{1,0:T(8,128)(2,1)S(1)}, bf16[512,1536]{1,0:T(8,128)(2,1)}, u32[]{:S(2)}) copy-start(bf16[512,1536]{1,0:T(8,128)(2,1)} %param.15) | copy-start | bytes 4718596
  12.4 32.0 %copy-start.31 = (bf16[1536,384]{1,0:T(8,128)(2,1)S(1)}, bf16[1536,384]{1,0:T(8,128)(2,1)}, u32[]{:S(2)}) copy-start(bf16[1536,384]{1,0:T(8,128)(2,1)} %param.17) | copy-start | bytes 3538948
  40.0 12.8 %collective-permute-start.5 = (bf16[2,4,128,2,128]{4,2,3,1,0:T(8,128)(2,1)S(1)}, bf16[2,4,128,2,128]{4,2,3,1,0:T(8,128)(2,1)}, u32[]{:S(2)}, u32[]{:S(2)}) collective-permute-start(bf16[2,4,128,2,128]{4,2,3,1,0:T(8,128)(2,1)S(1)} %get-tuple-element.10), channel_id=1, source_target_pairs={{0,64},{4,68},{8,72},{12,76},{16,80},{20,84},{24,88},{28,92},{32,9... | collective-permute-start | bytes 1572872 | tf_op jit(solution)/shard_map/ppermute | solution.py:58
  43.0 23.0 %collective-permute-start.6 = (bf16[2,4,128,2,128]{4,2,3,1,0:T(8,128)(2,1)S(1)}, bf16[2,4,128,2,128]{4,2,3,1,0:T(8,128)(2,1)}, u32[]{:S(2)}, u32[]{:S(2)}) collective-permute-start(bf16[2,4,128,2,128]{4,2,3,1,0:T(8,128)(2,1)S(1)} %get-tuple-element.10), channel_id=1, source_target_pairs={{0,96},{4,100},{8,104},{12,108},{16,112},{20,116},{24,120},{28,124... | collective-permute-start | bytes 1572872 | tf_op jit(solution)/shard_map/ppermute | solution.py:58
  43.7 23.0 %collective-permute-start.4 = (bf16[2,4,128,2,128]{4,2,3,1,0:T(8,128)(2,1)S(1)}, bf16[2,4,128,2,128]{4,2,3,1,0:T(8,128)(2,1)}, u32[]{:S(2)}, u32[]{:S(2)}) collective-permute-start(bf16[2,4,128,2,128]{4,2,3,1,0:T(8,128)(2,1)S(1)} %get-tuple-element.10), channel_id=1, source_target_pairs={{0,32},{4,36},{8,40},{12,44},{16,48},{20,52},{24,56},{28,60},{32,6... | collective-permute-start | bytes 1572872 | tf_op jit(solution)/shard_map/ppermute | solution.py:58
  45.4 21.3 %copy-start.10 = (bf16[512,384]{0,1:T(8,128)(2,1)}, bf16[512,384]{0,1:T(8,128)(2,1)S(1)}, u32[]{:S(2)}) copy-start(bf16[512,384]{0,1:T(8,128)(2,1)S(1)} %fusion.54) | copy-start | bytes 1179652
  46.4 25.1 %copy-start.30 = (s32[32]{0:T(128)S(1)}, s32[32]{0:T(128)}, u32[]{:S(2)}) copy-start(s32[32]{0:T(128)} %param.23) | copy-start | bytes 388
  69.7 16.0 %collective-permute-start.7 = (bf16[32,128,2,128]{3,1,2,0:T(8,128)(2,1)}, bf16[32,128,2,128]{3,1,2,0:T(8,128)(2,1)}, u32[]{:S(2)}, u32[]{:S(2)}) collective-permute-start(bf16[32,128,2,128]{3,1,2,0:T(8,128)(2,1)} %bitcast.12), channel_id=1, source_target_pairs={{0,1},{1,0},{2,3},{3,2},{4,5},{5,4},{6,7},{7,6},{8,9},{9,8},{10,11... | collective-permute-start | bytes 6291464 | tf_op jit(solution)/shard_map/ppermute | solution.py:43
  85.6 56.9 %collective-permute-start.11 = (bf16[768,1536]{1,0:T(8,128)(2,1)}, bf16[768,1536]{1,0:T(8,128)(2,1)}, u32[]{:S(2)}, u32[]{:S(2)}) collective-permute-start(bf16[768,1536]{1,0:T(8,128)(2,1)} %pad_maximum_fusion), channel_id=1, source_target_pairs={{0,1},{1,0},{2,3},{3,2},{4,5},{5,4},{6,7},{7,6},{8,9},{9,8},{10,11... | collective-permute-start | bytes 7077896 | tf_op jit(solution)/shard_map/ppermute | solution.py:43
  108.8 11.8 %collective-permute-start.8 = (bf16[512,384]{0,1:T(8,128)(2,1)S(1)}, bf16[512,384]{0,1:T(8,128)(2,1)S(1)}, u32[]{:S(2)}, u32[]{:S(2)}) collective-permute-start(bf16[512,384]{0,1:T(8,128)(2,1)S(1)} %bitcast.122), channel_id=1, source_target_pairs={{0,2},{1,3},{2,0},{3,1},{4,6},{5,7},{6,4},{7,5},{8,10},{9,11},{10,... | collective-permute-start | bytes 1179656 | tf_op jit(solution)/shard_map/ppermute | solution.py:43
  121.6 21.0 %collective-permute-start.9 = (bf16[512,768]{0,1:T(8,128)(2,1)}, bf16[512,768]{0,1:T(8,128)(2,1)}, u32[]{:S(2)}, u32[]{:S(2)}) collective-permute-start(bf16[512,768]{0,1:T(8,128)(2,1)} %pad_maximum_fusion.5), channel_id=1, source_target_pairs={{0,1},{1,0},{2,3},{3,2},{4,5},{5,4},{6,7},{7,6},{8,9},{9,8},{10,11... | collective-permute-start | bytes 2359304 | tf_op jit(solution)/shard_map/ppermute | solution.py:43
  151.8 81.1 %all-to-all-start = ((bf16[32,32,1536]{2,1,0:T(8,128)(2,1)}), bf16[32,32,1536]{2,1,0:T(8,128)(2,1)S(1)}, u32[]{:S(2)}, u32[]{:S(2)}) async-start(bf16[32,32,1536]{2,1,0:T(8,128)(2,1)} %bitcast.118), calls=%async_computation | async-start | bytes 6291456 | tf_op jit(solution)/shard_map/all_to_all | solution.py:181
  157.4 50.9 %copy-start.16 = (bf16[1,192,1536]{2,1,0:T(8,128)(2,1)S(1)}, bf16[1,192,1536]{2,1,0:T(8,128)(2,1)}, u32[]{:S(2)}) copy-start(bf16[1,192,1536]{2,1,0:T(8,128)(2,1)} %param.27) | copy-start | bytes 1769476
  157.4 60.2 %copy-start.14 = (bf16[1,1536,192]{1,2,0:T(8,128)(2,1)S(1)}, bf16[1,1536,192]{1,2,0:T(8,128)(2,1)}, u32[]{:S(2)}) copy-start(bf16[1,1536,192]{1,2,0:T(8,128)(2,1)} %param.26) | copy-start | bytes 1769476
  157.5 47.5 %collective-permute-start.12 = (bf16[1536,192]{0,1:T(8,128)(2,1)}, bf16[1536,192]{0,1:T(8,128)(2,1)S(1)}, u32[]{:S(2)}, u32[]{:S(2)}) collective-permute-start(bf16[1536,192]{0,1:T(8,128)(2,1)} %bitcast.127), channel_id=1, source_target_pairs={{0,2},{1,3},{2,0},{3,1},{4,6},{5,7},{6,4},{7,5},{8,10},{9,11},{10,... | collective-permute-start | bytes 1769480 | tf_op jit(solution)/shard_map/ppermute | solution.py:43
  158.1 59.5 %collective-permute-start.14 = (bf16[1536,192]{0,1:T(8,128)(2,1)}, bf16[1536,192]{0,1:T(8,128)(2,1)S(1)}, u32[]{:S(2)}, u32[]{:S(2)}) collective-permute-start(bf16[1536,192]{0,1:T(8,128)(2,1)} %bitcast.130), channel_id=1, source_target_pairs={{0,2},{1,3},{2,0},{3,1},{4,6},{5,7},{6,4},{7,5},{8,10},{9,11},{10,... | collective-permute-start | bytes 1769480 | tf_op jit(solution)/shard_map/ppermute | solution.py:43
  206.3 26.6 %collective-permute-start.13 = (bf16[1536,384]{0,1:T(8,128)(2,1)S(1)}, bf16[1536,384]{0,1:T(8,128)(2,1)}, u32[]{:S(2)}, u32[]{:S(2)}) collective-permute-start(bf16[1536,384]{0,1:T(8,128)(2,1)S(1)} %pad_maximum_fusion.2), channel_id=1, source_target_pairs={{0,1},{1,0},{2,3},{3,2},{4,5},{5,4},{6,7},{7,6},{8,9},{9,8},{10,11... | collective-permute-start | bytes 3538952 | tf_op jit(solution)/shard_map/ppermute | solution.py:43
  208.3 21.9 %collective-permute-start.16 = (bf16[192,1536]{1,0:T(8,128)(2,1)S(1)}, bf16[192,1536]{1,0:T(8,128)(2,1)S(1)}, u32[]{:S(2)}, u32[]{:S(2)}) collective-permute-start(bf16[192,1536]{1,0:T(8,128)(2,1)S(1)} %bitcast.133), channel_id=1, source_target_pairs={{0,2},{1,3},{2,0},{3,1},{4,6},{5,7},{6,4},{7,5},{8,10},{9,11},{10,... | collective-permute-start | bytes 1769480 | tf_op jit(solution)/shard_map/ppermute | solution.py:43
  218.8 18.5 %collective-permute-start.15 = (bf16[1536,384]{0,1:T(8,128)(2,1)}, bf16[1536,384]{0,1:T(8,128)(2,1)}, u32[]{:S(2)}, u32[]{:S(2)}) collective-permute-start(bf16[1536,384]{0,1:T(8,128)(2,1)} %pad_maximum_fusion.3), channel_id=1, source_target_pairs={{0,1},{1,0},{2,3},{3,2},{4,5},{5,4},{6,7},{7,6},{8,9},{9,8},{10,11... | collective-permute-start | bytes 3538952 | tf_op jit(solution)/shard_map/ppermute | solution.py:43
  231.5 9.8 %collective-permute-start.17 = (bf16[384,1536]{1,0:T(8,128)(2,1)}, bf16[384,1536]{1,0:T(8,128)(2,1)}, u32[]{:S(2)}, u32[]{:S(2)}) collective-permute-start(bf16[384,1536]{1,0:T(8,128)(2,1)} %pad_maximum_fusion.4), channel_id=1, source_target_pairs={{0,1},{1,0},{2,3},{3,2},{4,5},{5,4},{6,7},{7,6},{8,9},{9,8},{10,11... | collective-permute-start | bytes 3538952 | tf_op jit(solution)/shard_map/ppermute | solution.py:43
  246.9 51.0 %all-to-all-start.1 = ((bf16[32,32,1536]{2,1,0:T(8,128)(2,1)}), bf16[32,32,1536]{2,1,0:T(8,128)(2,1)S(1)}, u32[]{:S(2)}, u32[]{:S(2)}) async-start(bf16[32,32,1536]{2,1,0:T(8,128)(2,1)} %bitcast.121), calls=%async_computation.1 | async-start | bytes 6291456 | tf_op jit(solution)/shard_map/all_to_all | solution.py:188
  306.5 4.6 %collective-permute-start.18 = (f32[256,1536]{1,0:T(8,128)S(1)}, f32[256,1536]{1,0:T(8,128)S(1)}, u32[]{:S(2)}, u32[]{:S(2)}) collective-permute-start(f32[256,1536]{1,0:T(8,128)S(1)} %constant_dynamic-slice_fusion.1), channel_id=1, source_target_pairs={{0,1},{1,0},{2,3},{3,2},{4,5},{5,4},{6,7},{7,6},{8,9},{9,8},{10,11... | collective-permute-start | bytes 4718600 | tf_op jit(solution)/shard_map/ppermute | solution.py:43
  312.8 21.2 %collective-permute-start.19 = (f32[128,1536]{1,0:T(8,128)S(1)}, f32[128,1536]{1,0:T(8,128)S(1)}, u32[]{:S(2)}, u32[]{:S(2)}) collective-permute-start(f32[128,1536]{1,0:T(8,128)S(1)} %constant_dynamic-slice_fusion), channel_id=1, source_target_pairs={{0,2},{1,3},{2,0},{3,1},{4,6},{5,7},{6,4},{7,5},{8,10},{9,11},{10,... | collective-permute-start | bytes 2359304 | tf_op jit(solution)/shard_map/ppermute | solution.py:43
  335.1 11.3 %collective-permute-start.20 = (bf16[128,1536]{1,0:T(8,128)(2,1)S(1)}, bf16[128,1536]{1,0:T(8,128)(2,1)S(1)}, u32[]{:S(2)}, u32[]{:S(2)}) collective-permute-start(bf16[128,1536]{1,0:T(8,128)(2,1)S(1)} %add_convert_fusion), channel_id=1, source_target_pairs={{0,2},{1,3},{2,0},{3,1},{4,6},{5,7},{6,4},{7,5},{8,10},{9,11},{10,... | collective-permute-start | bytes 1179656 | tf_op jit(solution)/shard_map/ppermute | solution.py:43
  346.6 3.8 %collective-permute-start.21 = (bf16[256,1536]{1,0:T(8,128)(2,1)S(1)}, bf16[256,1536]{1,0:T(8,128)(2,1)S(1)}, u32[]{:S(2)}, u32[]{:S(2)}) collective-permute-start(bf16[256,1536]{1,0:T(8,128)(2,1)S(1)} %maximum_select_fusion.3), channel_id=1, source_target_pairs={{0,1},{1,0},{2,3},{3,2},{4,5},{5,4},{6,7},{7,6},{8,9},{9,8},{10,11... | collective-permute-start | bytes 2359304 | tf_op jit(solution)/shard_map/ppermute | solution.py:43
  (26 other events, 144.2 us)
